TPU v7x, 32 devices: a whole 2x2x4 slice. The times are simulated.
32 devices in a mesh: row: 8 (over y, x, core), col: 4 (over z).
Axes of the slice: x: 2, y: 2, z: 4, core: 2. Of those that a mesh axis runs over, the one named last changes fastest.
Arguments:
- pair_rep: bfloat16 [128, 128, 128], P(('row', 'col')), may hold values from -16 to 16
- tile_mask: int32 [1, 1], replicated, may hold values from 0 to 1, as said below
- chain_ids: int32 [128], replicated, may hold values from 0 to 3, never falling along the last dimension, each value on 1 to 64 neighbouring positions
- chain_bias: float32 [2, 4], replicated, may hold values from -6 to 6
- row_project: bfloat16 [128, 512], replicated, may hold values from -0.5 to 0.5
- row_bias_proj: bfloat16 [128, 4], replicated, may hold values from -36 to 36
- row_output: bfloat16 [128, 128], replicated, may hold values from -0.5 to 0.5
- col_project: bfloat16 [128, 512], replicated, may hold values from -0.5 to 0.5
- col_bias_proj: bfloat16 [128, 4], replicated, may hold values from -36 to 36
- col_output: bfloat16 [128, 128], replicated, may hold values from -0.5 to 0.5
- tri_left: bfloat16 [128, 256], replicated, may hold values from -0.5 to 0.5
- tri_right: bfloat16 [128, 256], replicated, may hold values from -0.5 to 0.5
- tri_gate: bfloat16 [128, 128], replicated, may hold values from -0.5 to 0.5
- tri_output: bfloat16 [128, 128], replicated, may hold values from -1.5 to 1.5
Outputs:
- pair_out: bfloat16 [128, 128, 128], P('row', 'col')
Inputs may be any that keep to these rules, and one draw needn't show every extreme that they name: `tile_mask`: every diagonal entry is 1. `chain_ids`: chain numbers never fall along the residues.
All inputs are finite; a program needn't handle non-finite values.
Results may differ from a plain program's by a relative error of at most 0.018.
Values may be sent and summed in bfloat16 or wider, within the bound.
No kernel may reach another device: no remote copies, remote signals or barrier semaphores. Data moves between devices by JAX's collectives and lax.ppermute only.
A program may use at most 64 MiB of HBM per device.

v0:
```python
import jax
import jax.numpy as jnp
from jax import lax
from jax.sharding import PartitionSpec as P


def layer_norm(values):
    values = values.astype(jnp.float32)
    center = values - jnp.mean(values, axis=-1, keepdims=True)
    spread = jnp.mean(center * center, axis=-1, keepdims=True)
    return center * lax.rsqrt(spread + 1e-05)


def tile_rows(positions, tile_table, length):
    tile_count = tile_table.shape[0]
    tile_width = length // tile_count
    onehot = (positions[:, None] // tile_width == jnp.arange(tile_count)[None, :]).astype(
        jnp.float32
    )
    picked = jnp.dot(onehot, tile_table.astype(jnp.float32))
    spread_out = jnp.broadcast_to(picked[:, :, None], (positions.shape[0], tile_count, tile_width))
    return spread_out.reshape(positions.shape[0], length) > 0.5


def tile_pairs(row_pos, col_pos, tile_table, length):
    tile_count = tile_table.shape[0]
    tile_width = length // tile_count
    row_hot = (row_pos[:, None] // tile_width == jnp.arange(tile_count)[None, :]).astype(
        jnp.float32
    )
    col_hot = (col_pos[:, None] // tile_width == jnp.arange(tile_count)[None, :]).astype(
        jnp.float32
    )
    return jnp.dot(jnp.dot(row_hot, tile_table.astype(jnp.float32)), col_hot.T)


def attend_lines(
    queries,
    key_rows,
    value_rows,
    gate_pre,
    bias_all,
    key_ok,
    chain_ids,
    chain_add,
    line_dim,
    flipped,
):
    line_count = queries.shape[line_dim]
    length = queries.shape[1 - line_dim]
    head_count = queries.shape[2]
    head_size = queries.shape[3]
    width_all = head_count * head_size
    query_rows = min(128, length)
    per_line = length // query_rows
    scaling = head_size ** (-0.5)

    def one_block(block_index):
        line_index = block_index // per_line
        offset = block_index % per_line * query_rows
        query_line = lax.dynamic_index_in_dim(queries, line_index, line_dim, keepdims=False)
        query_block = lax.dynamic_slice_in_dim(query_line, offset, query_rows, 0)
        key_line = lax.dynamic_index_in_dim(key_rows, line_index, line_dim, keepdims=False)
        value_line = lax.dynamic_index_in_dim(value_rows, line_index, line_dim, keepdims=False)
        scores = (
            jnp.einsum("qhd,khd->hqk", query_block, key_line, preferred_element_type=jnp.float32)
            * scaling
        )
        if flipped:
            bias_block = lax.dynamic_slice_in_dim(bias_all, offset, query_rows, 2).transpose(
                0, 2, 1
            )
        else:
            bias_block = lax.dynamic_slice_in_dim(bias_all, offset, query_rows, 1)
        scores = scores + bias_block
        chain_block = lax.dynamic_slice_in_dim(chain_ids, offset, query_rows, 0)
        same_chain = (chain_block[:, None] == chain_ids[None, :]).astype(jnp.float32)
        scores = scores + chain_add[:, None, None] * same_chain[None]
        usable = lax.dynamic_index_in_dim(key_ok, line_index, 0, keepdims=False)
        scores = jnp.where(usable[None, None, :], scores, -1000000000.0)
        row_peak = jnp.max(scores, axis=-1, keepdims=True)
        weights = jnp.exp(scores - row_peak)
        attention = (weights / jnp.sum(weights, axis=-1, keepdims=True)).astype(jnp.bfloat16)
        mixed_rows = jnp.einsum(
            "hqk,khd->qhd", attention, value_line, preferred_element_type=jnp.float32
        ).reshape(query_rows, width_all)
        gate_line = lax.dynamic_index_in_dim(gate_pre, line_index, line_dim, keepdims=False)
        gate_block = lax.dynamic_slice_in_dim(gate_line, offset, query_rows, 0)
        return (mixed_rows * jax.nn.sigmoid(gate_block)).astype(jnp.bfloat16)

    outputs = lax.map(one_block, jnp.arange(line_count * per_line, dtype=jnp.int32))
    outputs = outputs.reshape(line_count, length, width_all)
    if line_dim == 1:
        outputs = outputs.transpose(1, 0, 2)
    return outputs


def tri_acts(normed, weights, allowed):
    channels = normed.shape[-1]
    projected = jnp.dot(normed.reshape(-1, channels), weights, preferred_element_type=jnp.float32)
    projected = projected.reshape(normed.shape[0], normed.shape[1], 2 * channels)
    return (
        jax.nn.sigmoid(projected[..., channels:]) * projected[..., :channels] * allowed[..., None]
    ).astype(jnp.bfloat16)


def gather_lines(piece):
    device_count = lax.axis_size("row") * lax.axis_size("col")
    sent = jnp.broadcast_to(piece[None], (device_count,) + piece.shape)
    got = lax.all_to_all(sent, ("row", "col"), 0, 0, tiled=True)
    heads, rows_here, length = piece.shape
    return got.transpose(1, 0, 2, 3).reshape(heads, device_count * rows_here, length)


def shards(
    pair_rep,
    tile_mask,
    chain_ids,
    chain_bias,
    row_project,
    row_bias_proj,
    row_output,
    col_project,
    col_bias_proj,
    col_output,
    tri_left,
    tri_right,
    tri_gate,
    tri_output,
):
    n_row = lax.axis_size("row")
    n_col = lax.axis_size("col")
    device_count = n_row * n_col
    rows_here, length, channels = pair_rep.shape
    head_count = row_bias_proj.shape[1]
    head_size = channels // head_count
    row_index = lax.axis_index("row")
    col_index = lax.axis_index("col")
    device_index = row_index * n_col + col_index
    block_rows = length // n_row
    block_cols = length // n_col
    local_lines = device_index * rows_here + jnp.arange(rows_here, dtype=jnp.int32)
    local_cols = (
        col_index * block_cols + row_index * rows_here + jnp.arange(rows_here, dtype=jnp.int32)
    )
    normed = layer_norm(pair_rep).astype(jnp.bfloat16)
    flat_rows = normed.reshape(rows_here * length, channels)
    bias_rows = jnp.dot(flat_rows, row_bias_proj, preferred_element_type=jnp.float32)
    bias_rows = bias_rows.reshape(rows_here, length, head_count).transpose(2, 0, 1)
    bias_all = gather_lines(bias_rows)
    projected = jnp.dot(flat_rows, row_project, preferred_element_type=jnp.float32).reshape(
        rows_here, length, 4 * channels
    )
    qkv_rows = (
        projected[..., : 3 * channels]
        .astype(jnp.bfloat16)
        .reshape(rows_here, length, 3, head_count, head_size)
    )
    key_ok = tile_rows(local_lines, tile_mask, length)
    mixed_rows = attend_lines(
        qkv_rows[:, :, 0],
        qkv_rows[:, :, 1],
        qkv_rows[:, :, 2],
        projected[..., 3 * channels :],
        bias_all,
        key_ok,
        chain_ids,
        chain_bias[0],
        0,
        False,
    )
    update = jnp.dot(
        mixed_rows.reshape(-1, channels), row_output, preferred_element_type=jnp.float32
    ).reshape(rows_here, length, channels)
    first_pair = (pair_rep.astype(jnp.float32) + update).astype(jnp.bfloat16)
    normed_first = layer_norm(first_pair).astype(jnp.bfloat16)
    bias_next = jnp.dot(
        normed_first.reshape(-1, channels), col_bias_proj, preferred_element_type=jnp.float32
    )
    bias_next = bias_next.reshape(rows_here, length, head_count).transpose(2, 0, 1)
    bias_cols = gather_lines(bias_next)
    first_sent = (
        first_pair.reshape(rows_here, n_col, n_row, rows_here, channels)
        .transpose(0, 2, 1, 3, 4)
        .reshape(rows_here, length, channels)
    )
    columns = lax.all_to_all(first_sent, ("row", "col"), split_axis=1, concat_axis=0, tiled=True)
    normed_cols = layer_norm(columns).astype(jnp.bfloat16)
    projected_cols = jnp.dot(
        normed_cols.reshape(-1, channels), col_project, preferred_element_type=jnp.float32
    ).reshape(length, rows_here, 4 * channels)
    qkv_cols = (
        projected_cols[..., : 3 * channels]
        .astype(jnp.bfloat16)
        .reshape(length, rows_here, 3, head_count, head_size)
    )
    col_ok = tile_rows(local_cols, tile_mask.T, length)
    mixed_cols = attend_lines(
        qkv_cols[:, :, 0],
        qkv_cols[:, :, 1],
        qkv_cols[:, :, 2],
        projected_cols[..., 3 * channels :],
        bias_cols,
        col_ok,
        chain_ids,
        chain_bias[1],
        1,
        True,
    )
    update_cols = jnp.dot(
        mixed_cols.reshape(-1, channels), col_output, preferred_element_type=jnp.float32
    ).reshape(length, rows_here, channels)
    second_pair = (columns.astype(jnp.float32) + update_cols).astype(jnp.bfloat16)
    normed_second = layer_norm(second_pair).astype(jnp.bfloat16)
    edge_mask = tile_pairs(jnp.arange(length, dtype=jnp.int32), local_cols, tile_mask, length)
    left_all = tri_acts(normed_second, tri_left, edge_mask)
    right_all = tri_acts(normed_second, tri_right, edge_mask)
    raw_got = lax.all_to_all(
        second_pair.reshape(n_row, block_rows, rows_here, channels), "row", 0, 0, tiled=True
    )
    own_pair = raw_got.transpose(1, 0, 2, 3).reshape(block_rows, block_cols, channels)
    left_send = jnp.broadcast_to(
        left_all.reshape(n_row, 1, block_rows, rows_here, channels),
        (n_row, n_col, block_rows, rows_here, channels),
    )
    right_send = jnp.broadcast_to(
        right_all.reshape(1, n_col, block_cols, rows_here, channels),
        (n_row, n_col, block_cols, rows_here, channels),
    )
    outgoing = jnp.concatenate([left_send, right_send], axis=2).reshape(
        device_count, block_rows + block_cols, rows_here, channels
    )
    received = lax.all_to_all(outgoing, ("row", "col"), split_axis=0, concat_axis=0, tiled=True)
    product_sum = jnp.einsum(
        "sikc,sjkc->ijc",
        received[:, :block_rows],
        received[:, block_rows:],
        preferred_element_type=jnp.float32,
    )
    normed_own = layer_norm(own_pair).astype(jnp.bfloat16)
    gate_values = jax.nn.sigmoid(
        jnp.dot(normed_own.reshape(-1, channels), tri_gate, preferred_element_type=jnp.float32)
    ).reshape(block_rows, block_cols, channels)
    centered = layer_norm(product_sum).astype(jnp.bfloat16)
    update_tri = jnp.dot(
        centered.reshape(-1, channels), tri_output, preferred_element_type=jnp.float32
    ).reshape(block_rows, block_cols, channels)
    return (own_pair.astype(jnp.float32) + gate_values * update_tri).astype(jnp.bfloat16)


def solution(mesh):
    return jax.shard_map(
        shards,
        mesh=mesh,
        in_specs=(
            P(("row", "col"), None, None),
            P(),
            P(),
            P(),
            P(),
            P(),
            P(),
            P(),
            P(),
            P(),
            P(),
            P(),
            P(),
            P(),
        ),
        out_specs=P("row", "col", None),
        check_vma=False,
    )
```

profile of v0, /device:TPU:1, one launch (start us, length us, event | category | flops | bytes accessed | tf_op | source)
XLA Modules:
  0.0 142.1 jit_solution(1615348873690497271)
XLA Ops:
  0.0 1.1 convert_reduce_fusion
  1.1 1.1 fusion.48
  2.2 1.2 convolution_bitcast_fusion.2
  3.5 0.7 broadcast_in_dim.69
  4.2 7.1 %all-to-all-start = ((f32[32,4,4,128]{3,2,1,0:T(4,128)}), f32[32,4,4,128]{3,2,1,0:T(4,128)S(1)}, u32[]{:S(2)}, u32[]{:S(2)}) async-start(f32[32,4,4,128]{3,2,1,0:T(4,128)} %broadcast_in_dim.69), calls=%async_computation | async-start | bytes 524288 | tf_op jit(solution)/shard_map/all_to_all | solution.py:110
  12.0 1.3 fusion.70
  13.4 0.2 copy.140
  13.8 7.8 %all-to-all-done = f32[32,4,4,128]{3,2,1,0:T(4,128)S(1)} async-done(((f32[32,4,4,128]{3,2,1,0:T(4,128)}), f32[32,4,4,128]{3,2,1,0:T(4,128)S(1)}, u32[]{:S(2)}, u32[]{:S(2)}) %all-to-all-start) | async-done | bytes 262176 | tf_op jit(solution)/shard_map/all_to_all | solution.py:110
  21.9 14.2 %while.24 = (s32[]{:T(128)}, bf16[4,128,128]{1,2,0:T(8,128)(2,1)S(1)}, s32[4]{0:T(128)S(1)}, bf16[4,128,4,32]{1,3,2,0:T(8,128)(2,1)S(1)}, pred[4,128]{1,0:T(4,12...) while((s32[]{:T(128)}, ...), condition=%wide.region_5.6_spmd, body=%wide.region_2.5_spmd.sunk | while | flops 9159427 | bytes 2038723 | solution.py:91
  22.0 0.7 dynamic_slice.131
  24.8 0.2 fusion.127
  25.1 0.2 fusion.129
  25.5 0.7 dynamic_slice.131
  28.4 0.2 fusion.127
  28.7 0.2 fusion.129
  29.1 0.7 dynamic_slice.131
  31.9 0.2 fusion.127
  32.6 0.7 dynamic_slice.131
  35.5 0.2 fusion.127
  36.2 0.3 convert_reduce_fusion.2
  36.5 0.2 fusion.52
  36.8 0.8 copy.147
  37.6 2.6 %all-to-all-start.1 = ((bf16[4,128,128]{2,0,1:T(4,128)(2,1)}), bf16[4,128,128]{2,0,1:T(4,128)(2,1)S(1)}, u32[]{:S(2)}, u32[]{:S(2)}) async-start(bf16[4,128,128]{2,0,1:T(4,128)(2,1)} %copy.147), calls=%async_computation.1 | async-start | bytes 262144 | tf_op jit(solution)/shard_map/all_to_all | solution.py:187
  40.2 0.3 convolution_bitcast_fusion.1
  40.5 7.0 %all-to-all-done.1 = bf16[4,128,128]{2,0,1:T(4,128)(2,1)S(1)} async-done(((bf16[4,128,128]{2,0,1:T(4,128)(2,1)}), bf16[4,128,128]{2,0,1:T(4,128)(2,1)S(1)}, u32[]{:S(2)}, u32[]{:S(2)}) %all-to-all-start.1) | async-done | bytes 131104 | tf_op jit(solution)/shard_map/all_to_all | solution.py:187
  47.5 0.7 broadcast_in_dim.70
  48.3 3.5 %all-to-all-start.2 = ((f32[32,4,4,128]{3,2,1,0:T(4,128)}), f32[32,4,4,128]{3,2,1,0:T(4,128)S(1)}, u32[]{:S(2)}, u32[]{:S(2)}) async-start(f32[32,4,4,128]{3,2,1,0:T(4,128)} %broadcast_in_dim.70), calls=%async_computation.2 | async-start | bytes 524288 | tf_op jit(solution)/shard_map/all_to_all | solution.py:110
  51.8 0.2 fusion.66
  52.0 0.4 multiply_reduce_fusion.2
  52.4 0.3 copy.151
  52.8 0.3 copy.154
  53.5 0.4 fusion.64
  54.0 0.2 copy.155
  54.3 7.9 %all-to-all-done.2 = f32[32,4,4,128]{3,2,1,0:T(4,128)S(1)} async-done(((f32[32,4,4,128]{3,2,1,0:T(4,128)}), f32[32,4,4,128]{3,2,1,0:T(4,128)S(1)}, u32[]{:S(2)}, u32[]{:S(2)}) %all-to-all-start.2) | async-done | bytes 262176 | tf_op jit(solution)/shard_map/all_to_all | solution.py:110
  62.4 13.3 %while.25 = (s32[]{:T(128)}, bf16[4,128,128]{1,2,0:T(8,128)(2,1)S(1)}, s32[4]{0:T(128)S(1)}, bf16[128,4,4,32]{0,3,2,1:T(8,128)(2,1)S(1)}, pred[4,128]{1,0:T(4,12...) while((s32[]{:T(128)}, ...), condition=%wide.region_13.14_spmd, body=%wide.region_10.13_spmd.sunk | while | flops 9159427 | bytes 2038723 | solution.py:91
  62.4 0.6 dynamic_slice.137
  65.0 0.2 fusion.135
  65.7 0.6 dynamic_slice.137
  68.4 0.2 fusion.135
  68.7 0.2 fusion.137
  69.1 0.6 dynamic_slice.137
  71.7 0.2 fusion.135
  72.4 0.6 dynamic_slice.137
  75.0 0.2 fusion.135
  75.7 0.3 convert_reduce_fusion.1
  76.1 0.2 fusion.50
  76.4 0.3 fusion.78
  76.7 0.3 fusion.80
  77.2 0.8 copy.160
  78.0 3.4 %all-to-all-start.3 = ((bf16[8,16,4,128]{3,2,1,0:T(4,128)(2,1)}), bf16[8,16,4,128]{3,2,1,0:T(4,128)(2,1)S(1)}, u32[]{:S(2)}, u32[]{:S(2)}) async-start(bf16[8,16,4,128]{3,2,1,0:T(4,128)(2,1)} %copy.160), calls=%async_computation.3 | async-start | bytes 262144 | tf_op jit(solution)/shard_map/all_to_all | solution.py:218
  81.4 0.2 broadcast_in_dim.114
  81.8 1.3 pad_maximum_fusion
  83.1 2.9 %all-to-all-done.3 = bf16[8,16,4,128]{3,2,1,0:T(4,128)(2,1)S(1)} async-done(((bf16[8,16,4,128]{3,2,1,0:T(4,128)(2,1)}), bf16[8,16,4,128]{3,2,1,0:T(4,128)(2,1)S(1)}, u32[]{:S(2)}, u32[]{:S(2)}) %all-to-all-start.3) | async-done | bytes 131104 | tf_op jit(solution)/shard_map/all_to_all | solution.py:218
  86.0 3.4 %all-to-all-start.4 = ((bf16[32,48,4,128]{3,1,2,0:T(8,128)(2,1)}), bf16[32,48,4,128]{3,1,2,0:T(8,128)(2,1)S(1)}, u32[]{:S(2)}, u32[]{:S(2)}) async-start(bf16[32,48,4,128]{3,1,2,0:T(8,128)(2,1)} %bitcast.57), calls=%async_computation.4 | async-start | bytes 3145728 | tf_op jit(solution)/shard_map/all_to_all | solution.py:233
  89.4 0.2 fusion.65
  90.0 0.4 multiply_reduce_fusion.1
  91.0 0.3 fusion.37
  91.4 35.6 %all-to-all-done.4 = bf16[32,48,4,128]{3,1,2,0:T(8,128)(2,1)S(1)} async-done(((bf16[32,48,4,128]{3,1,2,0:T(8,128)(2,1)}), bf16[32,48,4,128]{3,1,2,0:T(8,128)(2,1)S(1)}, u32[]{:S(2)}, u32[]{:S(2)}) %all-to-all-start.4) | async-done | bytes 1572896 | tf_op jit(solution)/shard_map/all_to_all | solution.py:233
  127.0 6.4 %copy.181 = bf16[32,32,4,128]{1,0,2,3:T(8,128)(2,1)} copy(bf16[32,32,4,128]{3,1,2,0:T(8,128)(2,1)S(1)} %slice.89) | data formatting | bytes 2097152
  133.4 3.2 %copy.180 = bf16[32,16,4,128]{0,1,2,3:T(8,128)(2,1)S(1)} copy(bf16[32,16,4,128]{3,1,2,0:T(8,128)(2,1)S(1)} %slice.88) | data formatting | bytes 1048576
  136.7 3.7 %fusion.97 = (f32[16,32]{1,0:T(8,128)S(1)}, f32[16,32,128]{1,0,2:T(8,128)S(1)}) fusion(bf16[32,16,4,128]{0,1,2,3:T(8,128)(2,1)S(1)} %copy.180, bf16[32,32,4,128]{1,0,2,3:T(8,128)(2,1)} %copy.181), kind=kOutput, calls=%fused_computation.169 | convolution fusion | flops 16842240 | bytes 1837056 | tf_op jit(solution)/shard_map/sikc,sjkc->ijc/dot_general | solution.py:234
  140.4 0.2 multiply_reduce_fusion
  140.7 0.4 copy-done.7
  141.2 1.0 fusion.40
  (133 shorter events, 6.4 us)
Async XLA Ops:
  0.0 12.0 %copy-start = (bf16[128,512]{1,0:T(8,128)(2,1)S(1)}, bf16[128,512]{1,0:T(8,128)(2,1)}, u32[]{:S(2)}) copy-start(bf16[128,512]{1,0:T(8,128)(2,1)} %param.22) | copy-start | bytes 393220
  0.0 13.3 %copy-start.9 = (f32[2,4]{1,0:T(2,128)S(1)}, f32[2,4]{1,0:T(2,128)}, u32[]{:S(2)}) copy-start(f32[2,4]{1,0:T(2,128)} %param.21) | copy-start | bytes 100
  4.2 17.4 %all-to-all-start = ((f32[32,4,4,128]{3,2,1,0:T(4,128)}), f32[32,4,4,128]{3,2,1,0:T(4,128)S(1)}, u32[]{:S(2)}, u32[]{:S(2)}) async-start(f32[32,4,4,128]{3,2,1,0:T(4,128)} %broadcast_in_dim.69), calls=%async_computation | async-start | bytes 524288 | tf_op jit(solution)/shard_map/all_to_all | solution.py:110
  13.3 8.6 %copy-start.2 = (s32[128]{0:T(128)S(1)}, s32[128]{0:T(128)}, u32[]{:S(2)}) copy-start(s32[128]{0:T(128)} %param.20) | copy-start | bytes 1540
  21.9 14.2 %copy-start.1 = (bf16[4,128,128]{2,1,0:T(8,128)(2,1)S(1)}, bf16[4,128,128]{2,1,0:T(8,128)(2,1)}, u32[]{:S(2)}) copy-start(bf16[4,128,128]{2,1,0:T(8,128)(2,1)} %param.18) | copy-start | bytes 393220
  21.9 14.2 %copy-start.8 = (bf16[128,128]{1,0:T(8,128)(2,1)S(1)}, bf16[128,128]{1,0:T(8,128)(2,1)}, u32[]{:S(2)}) copy-start(bf16[128,128]{1,0:T(8,128)(2,1)} %param.24) | copy-start | bytes 98308
  21.9 18.3 %copy-start.11 = (bf16[128,4]{0,1:T(4,128)(2,1)S(1)}, bf16[128,4]{0,1:T(4,128)(2,1)}, u32[]{:S(2)}) copy-start(bf16[128,4]{0,1:T(4,128)(2,1)} %param.26) | copy-start | bytes 3076
  36.8 16.7 %copy-start.3 = (bf16[128,512]{1,0:T(8,128)(2,1)S(1)}, bf16[128,512]{1,0:T(8,128)(2,1)}, u32[]{:S(2)}) copy-start(bf16[128,512]{1,0:T(8,128)(2,1)} %param.25) | copy-start | bytes 393220
  37.6 9.9 %all-to-all-start.1 = ((bf16[4,128,128]{2,0,1:T(4,128)(2,1)}), bf16[4,128,128]{2,0,1:T(4,128)(2,1)S(1)}, u32[]{:S(2)}, u32[]{:S(2)}) async-start(bf16[4,128,128]{2,0,1:T(4,128)(2,1)} %copy.147), calls=%async_computation.1 | async-start | bytes 262144 | tf_op jit(solution)/shard_map/all_to_all | solution.py:187
  48.3 13.9 %all-to-all-start.2 = ((f32[32,4,4,128]{3,2,1,0:T(4,128)}), f32[32,4,4,128]{3,2,1,0:T(4,128)S(1)}, u32[]{:S(2)}, u32[]{:S(2)}) async-start(f32[32,4,4,128]{3,2,1,0:T(4,128)} %broadcast_in_dim.70), calls=%async_computation.2 | async-start | bytes 524288 | tf_op jit(solution)/shard_map/all_to_all | solution.py:110
  62.3 13.4 %copy-start.6 = (bf16[128,128]{1,0:T(8,128)(2,1)S(1)}, bf16[128,128]{1,0:T(8,128)(2,1)}, u32[]{:S(2)}) copy-start(bf16[128,128]{1,0:T(8,128)(2,1)} %param.27) | copy-start | bytes 98308
  62.3 14.0 %copy-start.4 = (bf16[128,256]{1,0:T(8,128)(2,1)S(1)}, bf16[128,256]{1,0:T(8,128)(2,1)}, u32[]{:S(2)}) copy-start(bf16[128,256]{1,0:T(8,128)(2,1)} %param.29) | copy-start | bytes 196612
  62.4 14.3 %copy-start.5 = (bf16[128,256]{1,0:T(8,128)(2,1)S(1)}, bf16[128,256]{1,0:T(8,128)(2,1)}, u32[]{:S(2)}) copy-start(bf16[128,256]{1,0:T(8,128)(2,1)} %param.28) | copy-start | bytes 196612
  78.0 8.0 %all-to-all-start.3 = ((bf16[8,16,4,128]{3,2,1,0:T(4,128)(2,1)}), bf16[8,16,4,128]{3,2,1,0:T(4,128)(2,1)S(1)}, u32[]{:S(2)}, u32[]{:S(2)}) async-start(bf16[8,16,4,128]{3,2,1,0:T(4,128)(2,1)} %copy.160), calls=%async_computation.3 | async-start | bytes 262144 | tf_op jit(solution)/shard_map/all_to_all | solution.py:218
  86.0 5.0 %copy-start.10 = (bf16[128,128]{1,0:T(8,128)(2,1)S(1)}, bf16[128,128]{1,0:T(8,128)(2,1)}, u32[]{:S(2)}) copy-start(bf16[128,128]{1,0:T(8,128)(2,1)} %param.30) | copy-start | bytes 98308
  86.0 40.9 %all-to-all-start.4 = ((bf16[32,48,4,128]{3,1,2,0:T(8,128)(2,1)}), bf16[32,48,4,128]{3,1,2,0:T(8,128)(2,1)S(1)}, u32[]{:S(2)}, u32[]{:S(2)}) async-start(bf16[32,48,4,128]{3,1,2,0:T(8,128)(2,1)} %bitcast.57), calls=%async_computation.4 | async-start | bytes 3145728 | tf_op jit(solution)/shard_map/all_to_all | solution.py:233
  140.4 0.8 copy-start.7
where the time goes:
time: 143 us; the launch traced here: 142 us
  waiting for transfers between devices  61.3 us (43%)
  local copies, waits for them, and re-layouts  22.5 us (16%)
  starting transfers between devices  19.9 us (14%)
  loops' own time  16.5 us (12%)
  matrix products  13 us (9%)
  other arithmetic  7.65 us (5%)
    all_to_all x1, waiting for transfers between devices, shards(): lax.all_to_all(outgoing, ('row', 'col'), split_axis=0, concat_axis=0, til...  35.6 us
    another operation x2, loops' own time, attend_lines(): lax.map(one_block, jnp.arange(line_count * per_line, dtype=jnp.int32))  16.5 us
    all_to_all x2, waiting for transfers between devices, gather_lines(): got = lax.all_to_all(sent, ('row', 'col'), 0, 0, tiled=True)  15.8 us
    all_to_all x2, starting transfers between devices, gather_lines(): got = lax.all_to_all(sent, ('row', 'col'), 0, 0, tiled=True)  10.5 us
    unnamed x26, local copies, waits for them, and re-layouts  10.1 us
    all_to_all x1, waiting for transfers between devices, shards(): lax.all_to_all(first_sent, ('row', 'col'), split_axis=1, concat_axis=0, t...  7.03 us
    dynamic_slice x8, local copies, waits for them, and re-layouts, attend_lines(): lax.map(one_block, jnp.arange(line_count * per_line, dtype=jnp.int32))  5.01 us
    dot_general x1, matrix products, shards(): jnp.einsum('sikc,sjkc->ijc', received[:, :block_rows], received[:, block_...  3.72 us
  transfers between devices with their start and end apart: 5, of which 5 were waited for; matrix products, arithmetic and copies ran while one was open for 6% of the time, Pallas kernels for 0%

commit v1 on v0

--- a/solution.py
+++ b/solution.py
@@ -1,7 +1,31 @@
+import functools
 import jax
 import jax.numpy as jnp
 from jax import lax
 from jax.sharding import PartitionSpec as P
+
+
+def attach_the_tokens(shard_in, lane_axis):
+    lower, moved = (jax.lax.axis_size(lane_axis), jax.lax.axis_index(lane_axis))
+    met_up = shard_in.shape[0] // lower
+    row_out = list(shard_in.shape)
+    row_out[0] = met_up
+    base_arr = row_out[0]
+    row_out[0] = base_arr * lower
+    m = 0
+    y2 = jnp.zeros(row_out, shard_in.dtype)
+    while m < lower:
+        current_arr = lax.dynamic_slice_in_dim(shard_in, (moved ^ m) * met_up, met_up, axis=0)
+        if m:
+            current_arr = jax.lax.ppermute(
+                current_arr, lane_axis, tuple(((i0, i0 ^ m) for i0 in range(lower)))
+            )
+        y2 = lax.dynamic_update_slice_in_dim(y2, current_arr, (moved ^ m) * base_arr, axis=0)
+        m += 1
+    return y2
+
+
+quarters_press = functools.partial(attach_the_tokens, lane_axis="row")
 
 
 def layer_norm(values):
@@ -215,9 +239,7 @@
     edge_mask = tile_pairs(jnp.arange(length, dtype=jnp.int32), local_cols, tile_mask, length)
     left_all = tri_acts(normed_second, tri_left, edge_mask)
     right_all = tri_acts(normed_second, tri_right, edge_mask)
-    raw_got = lax.all_to_all(
-        second_pair.reshape(n_row, block_rows, rows_here, channels), "row", 0, 0, tiled=True
-    )
+    raw_got = quarters_press(second_pair.reshape(n_row, block_rows, rows_here, channels))
     own_pair = raw_got.transpose(1, 0, 2, 3).reshape(block_rows, block_cols, channels)
     left_send = jnp.broadcast_to(
         left_all.reshape(n_row, 1, block_rows, rows_here, channels),

time: 143 us -> 135 us (0.944)
  waiting for transfers between devices: 61.3 us -> 49.7 us
  starting transfers between devices: 19.9 us -> 24.7 us
    all_to_all x1, waiting for transfers between devices: 35.6 us -> 21 us  [shards(): lax.all_to_all(outgoing, ('row', 'col'), split_axis=0, concat_axis=0, til...]
    ppermute x0 -> x7, starting transfers between devices: none -> 8.9 us  [attach_the_tokens(): jax.lax.ppermute(current_arr, lane_axis, tuple(((i0, i0 ^ m) for i0 in ra...]
    ppermute x0 -> x7, waiting for transfers between devices: none -> 5.92 us  [attach_the_tokens(): jax.lax.ppermute(current_arr, lane_axis, tuple(((i0, i0 ^ m) for i0 in ra...]
    all_to_all x1 -> x0, starting transfers between devices: 3.44 us -> none  [shards(): lax.all_to_all(second_pair.reshape(n_row, block_rows, rows_here, channels...]
    all_to_all x1 -> x0, waiting for transfers between devices: 2.92 us -> none  [shards(): lax.all_to_all(second_pair.reshape(n_row, block_rows, rows_here, channels...]
  transfers between devices with their start and end apart: 5 -> 11, of which waited for: 5 -> 7; matrix products, arithmetic and copies ran while one was open for 6% -> 4% of each run, Pallas kernels for 0% -> 0%
where the time goes in v1:
time: 135 us; the launch traced here: 134 us
  waiting for transfers between devices  49.7 us (37%)
  starting transfers between devices  24.7 us (18%)
  local copies, waits for them, and re-layouts  21.3 us (16%)
  loops' own time  16.5 us (12%)
  matrix products  12.3 us (9%)
  other arithmetic  8.35 us (6%)
    all_to_all x1, waiting for transfers between devices, shards(): lax.all_to_all(outgoing, ('row', 'col'), split_axis=0, concat_axis=0, til...  21 us
    another operation x2, loops' own time, attend_lines(): lax.map(one_block, jnp.arange(line_count * per_line, dtype=jnp.int32))  16.5 us
    all_to_all x2, waiting for transfers between devices, gather_lines(): got = lax.all_to_all(sent, ('row', 'col'), 0, 0, tiled=True)  15.8 us
    all_to_all x2, starting transfers between devices, gather_lines(): got = lax.all_to_all(sent, ('row', 'col'), 0, 0, tiled=True)  10.5 us
    unnamed x26, local copies, waits for them, and re-layouts  10.1 us
    ppermute x7, starting transfers between devices, attach_the_tokens(): jax.lax.ppermute(current_arr, lane_axis, tuple(((i0, i0 ^ m) for i0 in ra...  8.9 us
    all_to_all x1, waiting for transfers between devices, shards(): lax.all_to_all(first_sent, ('row', 'col'), split_axis=1, concat_axis=0, t...  7.03 us
    ppermute x7, waiting for transfers between devices, attach_the_tokens(): jax.lax.ppermute(current_arr, lane_axis, tuple(((i0, i0 ^ m) for i0 in ra...  5.92 us
  transfers between devices with their start and end apart: 11, of which 7 were waited for; matrix products, arithmetic and copies ran while one was open for 4% of the time, Pallas kernels for 0%

profile of v1, /device:TPU:1, one launch (start us, length us, event | category | flops | bytes accessed | tf_op | source)
XLA Modules:
  0.0 134.3 jit_solution(12388107856718237065)
XLA Ops:
  0.0 1.1 convert_reduce_fusion
  1.1 1.1 fusion.46
  2.2 1.2 convolution_bitcast_fusion.2
  3.5 0.7 broadcast_in_dim.72
  4.2 7.1 %all-to-all-start = ((f32[32,4,4,128]{3,2,1,0:T(4,128)}), f32[32,4,4,128]{3,2,1,0:T(4,128)S(1)}, u32[]{:S(2)}, u32[]{:S(2)}) async-start(f32[32,4,4,128]{3,2,1,0:T(4,128)} %broadcast_in_dim.72), calls=%async_computation | async-start | bytes 524288 | tf_op jit(solution)/shard_map/all_to_all | solution.py:134
  12.0 1.3 fusion.69
  13.7 7.9 %all-to-all-done = f32[32,4,4,128]{3,2,1,0:T(4,128)S(1)} async-done(((f32[32,4,4,128]{3,2,1,0:T(4,128)}), f32[32,4,4,128]{3,2,1,0:T(4,128)S(1)}, u32[]{:S(2)}, u32[]{:S(2)}) %all-to-all-start) | async-done | bytes 262176 | tf_op jit(solution)/shard_map/all_to_all | solution.py:134
  21.9 14.2 %while.24 = (s32[]{:T(128)}, bf16[4,128,128]{1,2,0:T(8,128)(2,1)S(1)}, s32[4]{0:T(128)S(1)}, bf16[4,128,4,32]{1,3,2,0:T(8,128)(2,1)S(1)}, pred[4,128]{1,0:T(4,12...) while((s32[]{:T(128)}, ...), condition=%wide.region_5.6_spmd, body=%wide.region_2.5_spmd.sunk | while | flops 9159427 | bytes 2038723 | solution.py:115
  22.0 0.7 dynamic_slice.171
  24.8 0.2 fusion.126
  25.5 0.7 dynamic_slice.171
  28.4 0.2 fusion.126
  29.1 0.7 dynamic_slice.171
  31.9 0.2 fusion.126
  32.6 0.7 dynamic_slice.171
  35.5 0.2 fusion.126
  36.2 0.3 convert_reduce_fusion.2
  36.5 0.2 fusion.50
  36.8 0.8 copy.140
  37.6 2.6 %all-to-all-start.1 = ((bf16[4,128,128]{2,0,1:T(4,128)(2,1)}), bf16[4,128,128]{2,0,1:T(4,128)(2,1)S(1)}, u32[]{:S(2)}, u32[]{:S(2)}) async-start(bf16[4,128,128]{2,0,1:T(4,128)(2,1)} %copy.140), calls=%async_computation.1 | async-start | bytes 262144 | tf_op jit(solution)/shard_map/all_to_all | solution.py:211
  40.2 0.3 convolution_bitcast_fusion.1
  40.5 7.0 %all-to-all-done.1 = bf16[4,128,128]{2,0,1:T(4,128)(2,1)S(1)} async-done(((bf16[4,128,128]{2,0,1:T(4,128)(2,1)}), bf16[4,128,128]{2,0,1:T(4,128)(2,1)S(1)}, u32[]{:S(2)}, u32[]{:S(2)}) %all-to-all-start.1) | async-done | bytes 131104 | tf_op jit(solution)/shard_map/all_to_all | solution.py:211
  47.5 0.7 broadcast_in_dim.73
  48.3 3.5 %all-to-all-start.2 = ((f32[32,4,4,128]{3,2,1,0:T(4,128)}), f32[32,4,4,128]{3,2,1,0:T(4,128)S(1)}, u32[]{:S(2)}, u32[]{:S(2)}) async-start(f32[32,4,4,128]{3,2,1,0:T(4,128)} %broadcast_in_dim.73), calls=%async_computation.2 | async-start | bytes 524288 | tf_op jit(solution)/shard_map/all_to_all | solution.py:134
  52.0 0.4 multiply_reduce_fusion.1
  52.4 0.3 copy.144
  52.8 0.3 copy.147
  53.5 0.4 fusion.64
  54.2 7.9 %all-to-all-done.2 = f32[32,4,4,128]{3,2,1,0:T(4,128)S(1)} async-done(((f32[32,4,4,128]{3,2,1,0:T(4,128)}), f32[32,4,4,128]{3,2,1,0:T(4,128)S(1)}, u32[]{:S(2)}, u32[]{:S(2)}) %all-to-all-start.2) | async-done | bytes 262176 | tf_op jit(solution)/shard_map/all_to_all | solution.py:134
  62.4 13.3 %while.25 = (s32[]{:T(128)}, bf16[4,128,128]{1,2,0:T(8,128)(2,1)S(1)}, s32[4]{0:T(128)S(1)}, bf16[128,4,4,32]{0,3,2,1:T(8,128)(2,1)S(1)}, pred[4,128]{1,0:T(4,12...) while((s32[]{:T(128)}, ...), condition=%wide.region_13.14_spmd, body=%wide.region_10.13_spmd.sunk | while | flops 9159427 | bytes 2038723 | solution.py:115
  62.4 0.6 dynamic_slice.177
  65.0 0.2 fusion.134
  65.7 0.6 dynamic_slice.177
  68.4 0.2 fusion.134
  69.1 0.6 dynamic_slice.177
  71.7 0.2 fusion.134
  72.4 0.6 dynamic_slice.177
  75.0 0.2 fusion.134
  75.7 0.3 convert_reduce_fusion.1
  76.1 0.2 fusion.48
  76.4 0.3 fusion.77
  76.7 0.3 fusion.79
  77.2 0.2 broadcast_in_dim.118
  77.6 1.3 pad_maximum_fusion
  78.9 2.7 %all-to-all-start.3 = ((bf16[32,48,4,128]{3,1,2,0:T(8,128)(2,1)}), bf16[32,48,4,128]{3,1,2,0:T(8,128)(2,1)S(1)}, u32[]{:S(2)}, u32[]{:S(2)}) async-start(bf16[32,48,4,128]{3,1,2,0:T(8,128)(2,1)} %bitcast.57), calls=%async_computation.3 | async-start | bytes 3145728 | tf_op jit(solution)/shard_map/all_to_all | solution.py:255
  81.7 0.5 collective-permute-start
  82.2 1.2 collective-permute-start.1
  83.4 0.5 collective-permute-start.2
  83.9 1.2 collective-permute-start.3
  85.2 0.5 collective-permute-start.4
  85.8 2.2 %collective-permute-start.5 = (bf16[1,16,4,128]{3,1,0,2:T(8,128)(2,1)S(1)}, bf16[1,16,4,128]{3,1,0,2:T(8,128)(2,1)S(1)}, u32[]{:S(2)}, u32[]{:S(2)}) collective-permute-start(bf16[1,16,4,128]{3,1,0,2:T(8,128)(2,1)S(1)} %get-tuple-element.446), channel_id=1, source_target_pairs={{0,24},{4,28},{8,16},{12,20},{16,8},{20,12},{24,0},{28,4},{1,25},{... | collective-permute-start | bytes 49160 | tf_op jit(solution)/shard_map/ppermute | solution.py:20
  88.0 3.9 %collective-permute-done.1 = bf16[1,16,4,128]{3,1,0,2:T(8,128)(2,1)S(1)} collective-permute-done((bf16[1,16,4,128]{3,1,0,2:T(8,128)(2,1)S(1)}, bf16[1,16,4,128]{3,1,0,2:T(8,128)(2,1)S(1)}, u32[]{:S(2)}, u32[]{:S(2)}) %collective-permute-start.1) | collective-permute-done | bytes 16416 | tf_op jit(solution)/shard_map/ppermute | solution.py:20
  91.9 2.7 %collective-permute-start.6 = (bf16[1,16,4,128]{3,1,0,2:T(8,128)(2,1)S(1)}, bf16[1,16,4,128]{3,1,0,2:T(8,128)(2,1)S(1)}, u32[]{:S(2)}, u32[]{:S(2)}) collective-permute-start(bf16[1,16,4,128]{3,1,0,2:T(8,128)(2,1)S(1)} %get-tuple-element.445), channel_id=1, source_target_pairs={{0,28},{4,24},{8,20},{12,16},{16,12},{20,8},{24,4},{28,0},{1,29},{... | collective-permute-start | bytes 49160 | tf_op jit(solution)/shard_map/ppermute | solution.py:20
  94.8 1.2 collective-permute-done.4
  96.0 0.8 collective-permute-done.6
  97.2 0.4 fusion.63
  97.7 0.3 fusion.36
  98.0 21.0 %all-to-all-done.3 = bf16[32,48,4,128]{3,1,2,0:T(8,128)(2,1)S(1)} async-done(((bf16[32,48,4,128]{3,1,2,0:T(8,128)(2,1)}), bf16[32,48,4,128]{3,1,2,0:T(8,128)(2,1)S(1)}, u32[]{:S(2)}, u32[]{:S(2)}) %all-to-all-start.3) | async-done | bytes 1572896 | tf_op jit(solution)/shard_map/all_to_all | solution.py:255
  119.1 6.4 %copy.174 = bf16[32,32,4,128]{1,0,2,3:T(8,128)(2,1)} copy(bf16[32,32,4,128]{3,1,2,0:T(8,128)(2,1)S(1)} %slice.89) | data formatting | bytes 2097152
  125.5 3.2 %copy.173 = bf16[32,16,4,128]{0,1,2,3:T(8,128)(2,1)S(1)} copy(bf16[32,16,4,128]{3,1,2,0:T(8,128)(2,1)S(1)} %slice.88) | data formatting | bytes 1048576
  128.8 3.7 %fusion.96 = (f32[16,32]{1,0:T(8,128)S(1)}, f32[16,32,128]{1,0,2:T(8,128)S(1)}) fusion(bf16[32,16,4,128]{0,1,2,3:T(8,128)(2,1)S(1)} %copy.173, bf16[32,32,4,128]{1,0,2,3:T(8,128)(2,1)} %copy.174), kind=kOutput, calls=%fused_computation.185 | convolution fusion | flops 16842240 | bytes 1837056 | tf_op jit(solution)/shard_map/sikc,sjkc->ijc/dot_general | solution.py:256
  132.8 0.4 copy-done.7
  133.3 0.3 convolution_multiply_fusion.2
  133.6 0.7 add_convert_fusion
  (148 shorter events, 7.5 us)
Async XLA Ops:
  0.0 12.0 %copy-start = (bf16[128,512]{1,0:T(8,128)(2,1)S(1)}, bf16[128,512]{1,0:T(8,128)(2,1)}, u32[]{:S(2)}) copy-start(bf16[128,512]{1,0:T(8,128)(2,1)} %param.22) | copy-start | bytes 393220
  0.0 13.3 %copy-start.9 = (f32[2,4]{1,0:T(2,128)S(1)}, f32[2,4]{1,0:T(2,128)}, u32[]{:S(2)}) copy-start(f32[2,4]{1,0:T(2,128)} %param.21) | copy-start | bytes 100
  4.2 17.4 %all-to-all-start = ((f32[32,4,4,128]{3,2,1,0:T(4,128)}), f32[32,4,4,128]{3,2,1,0:T(4,128)S(1)}, u32[]{:S(2)}, u32[]{:S(2)}) async-start(f32[32,4,4,128]{3,2,1,0:T(4,128)} %broadcast_in_dim.72), calls=%async_computation | async-start | bytes 524288 | tf_op jit(solution)/shard_map/all_to_all | solution.py:134
  13.3 8.6 %copy-start.2 = (s32[128]{0:T(128)S(1)}, s32[128]{0:T(128)}, u32[]{:S(2)}) copy-start(s32[128]{0:T(128)} %param.20) | copy-start | bytes 1540
  21.9 14.2 %copy-start.1 = (bf16[4,128,128]{2,1,0:T(8,128)(2,1)S(1)}, bf16[4,128,128]{2,1,0:T(8,128)(2,1)}, u32[]{:S(2)}) copy-start(bf16[4,128,128]{2,1,0:T(8,128)(2,1)} %param.18) | copy-start | bytes 393220
  21.9 14.2 %copy-start.8 = (bf16[128,128]{1,0:T(8,128)(2,1)S(1)}, bf16[128,128]{1,0:T(8,128)(2,1)}, u32[]{:S(2)}) copy-start(bf16[128,128]{1,0:T(8,128)(2,1)} %param.24) | copy-start | bytes 98308
  21.9 18.3 %copy-start.11 = (bf16[128,4]{0,1:T(4,128)(2,1)S(1)}, bf16[128,4]{0,1:T(4,128)(2,1)}, u32[]{:S(2)}) copy-start(bf16[128,4]{0,1:T(4,128)(2,1)} %param.26) | copy-start | bytes 3076
  36.8 16.7 %copy-start.3 = (bf16[128,512]{1,0:T(8,128)(2,1)S(1)}, bf16[128,512]{1,0:T(8,128)(2,1)}, u32[]{:S(2)}) copy-start(bf16[128,512]{1,0:T(8,128)(2,1)} %param.25) | copy-start | bytes 393220
  37.6 9.9 %all-to-all-start.1 = ((bf16[4,128,128]{2,0,1:T(4,128)(2,1)}), bf16[4,128,128]{2,0,1:T(4,128)(2,1)S(1)}, u32[]{:S(2)}, u32[]{:S(2)}) async-start(bf16[4,128,128]{2,0,1:T(4,128)(2,1)} %copy.140), calls=%async_computation.1 | async-start | bytes 262144 | tf_op jit(solution)/shard_map/all_to_all | solution.py:211
  48.3 13.9 %all-to-all-start.2 = ((f32[32,4,4,128]{3,2,1,0:T(4,128)}), f32[32,4,4,128]{3,2,1,0:T(4,128)S(1)}, u32[]{:S(2)}, u32[]{:S(2)}) async-start(f32[32,4,4,128]{3,2,1,0:T(4,128)} %broadcast_in_dim.73), calls=%async_computation.2 | async-start | bytes 524288 | tf_op jit(solution)/shard_map/all_to_all | solution.py:134
  62.3 13.4 %copy-start.6 = (bf16[128,128]{1,0:T(8,128)(2,1)S(1)}, bf16[128,128]{1,0:T(8,128)(2,1)}, u32[]{:S(2)}) copy-start(bf16[128,128]{1,0:T(8,128)(2,1)} %param.27) | copy-start | bytes 98308
  62.3 14.0 %copy-start.4 = (bf16[128,256]{1,0:T(8,128)(2,1)S(1)}, bf16[128,256]{1,0:T(8,128)(2,1)}, u32[]{:S(2)}) copy-start(bf16[128,256]{1,0:T(8,128)(2,1)} %param.29) | copy-start | bytes 196612
  62.4 14.3 %copy-start.5 = (bf16[128,256]{1,0:T(8,128)(2,1)S(1)}, bf16[128,256]{1,0:T(8,128)(2,1)}, u32[]{:S(2)}) copy-start(bf16[128,256]{1,0:T(8,128)(2,1)} %param.28) | copy-start | bytes 196612
  78.9 18.8 %copy-start.10 = (bf16[128,128]{1,0:T(8,128)(2,1)S(1)}, bf16[128,128]{1,0:T(8,128)(2,1)}, u32[]{:S(2)}) copy-start(bf16[128,128]{1,0:T(8,128)(2,1)} %param.30) | copy-start | bytes 98308
  78.9 40.1 %all-to-all-start.3 = ((bf16[32,48,4,128]{3,1,2,0:T(8,128)(2,1)}), bf16[32,48,4,128]{3,1,2,0:T(8,128)(2,1)S(1)}, u32[]{:S(2)}, u32[]{:S(2)}) async-start(bf16[32,48,4,128]{3,1,2,0:T(8,128)(2,1)} %bitcast.57), calls=%async_computation.3 | async-start | bytes 3145728 | tf_op jit(solution)/shard_map/all_to_all | solution.py:255
  81.7 4.1 %collective-permute-start = (bf16[1,16,4,128]{3,1,0,2:T(8,128)(2,1)S(1)}, bf16[1,16,4,128]{3,1,0,2:T(8,128)(2,1)S(1)}, u32[]{:S(2)}, u32[]{:S(2)}) collective-permute-start(bf16[1,16,4,128]{3,1,0,2:T(8,128)(2,1)S(1)} %get-tuple-element.451), channel_id=1, source_target_pairs={{0,4},{4,0},{8,12},{12,8},{16,20},{20,16},{24,28},{28,24},{1,5},{5... | collective-permute-start | bytes 49160 | tf_op jit(solution)/shard_map/ppermute | solution.py:20
  82.2 9.7 %collective-permute-start.1 = (bf16[1,16,4,128]{3,1,0,2:T(8,128)(2,1)S(1)}, bf16[1,16,4,128]{3,1,0,2:T(8,128)(2,1)S(1)}, u32[]{:S(2)}, u32[]{:S(2)}) collective-permute-start(bf16[1,16,4,128]{3,1,0,2:T(8,128)(2,1)S(1)} %get-tuple-element.450), channel_id=1, source_target_pairs={{0,8},{4,12},{8,0},{12,4},{16,24},{20,28},{24,16},{28,20},{1,9},{5... | collective-permute-start | bytes 49160 | tf_op jit(solution)/shard_map/ppermute | solution.py:20
  83.4 11.3 %collective-permute-start.2 = (bf16[1,16,4,128]{3,1,0,2:T(8,128)(2,1)S(1)}, bf16[1,16,4,128]{3,1,0,2:T(8,128)(2,1)S(1)}, u32[]{:S(2)}, u32[]{:S(2)}) collective-permute-start(bf16[1,16,4,128]{3,1,0,2:T(8,128)(2,1)S(1)} %get-tuple-element.449), channel_id=1, source_target_pairs={{0,12},{4,8},{8,4},{12,0},{16,28},{20,24},{24,20},{28,16},{1,13},{... | collective-permute-start | bytes 49160 | tf_op jit(solution)/shard_map/ppermute | solution.py:20
  83.9 10.8 %collective-permute-start.3 = (bf16[1,16,4,128]{3,1,0,2:T(8,128)(2,1)S(1)}, bf16[1,16,4,128]{3,1,0,2:T(8,128)(2,1)S(1)}, u32[]{:S(2)}, u32[]{:S(2)}) collective-permute-start(bf16[1,16,4,128]{3,1,0,2:T(8,128)(2,1)S(1)} %get-tuple-element.448), channel_id=1, source_target_pairs={{0,16},{4,20},{8,24},{12,28},{16,0},{20,4},{24,8},{28,12},{1,17},{... | collective-permute-start | bytes 49160 | tf_op jit(solution)/shard_map/ppermute | solution.py:20
  85.2 10.8 %collective-permute-start.4 = (bf16[1,16,4,128]{3,1,0,2:T(8,128)(2,1)S(1)}, bf16[1,16,4,128]{3,1,0,2:T(8,128)(2,1)S(1)}, u32[]{:S(2)}, u32[]{:S(2)}) collective-permute-start(bf16[1,16,4,128]{3,1,0,2:T(8,128)(2,1)S(1)} %get-tuple-element.447), channel_id=1, source_target_pairs={{0,20},{4,16},{8,28},{12,24},{16,4},{20,0},{24,12},{28,8},{1,21},{... | collective-permute-start | bytes 49160 | tf_op jit(solution)/shard_map/ppermute | solution.py:20
  85.8 10.2 %collective-permute-start.5 = (bf16[1,16,4,128]{3,1,0,2:T(8,128)(2,1)S(1)}, bf16[1,16,4,128]{3,1,0,2:T(8,128)(2,1)S(1)}, u32[]{:S(2)}, u32[]{:S(2)}) collective-permute-start(bf16[1,16,4,128]{3,1,0,2:T(8,128)(2,1)S(1)} %get-tuple-element.446), channel_id=1, source_target_pairs={{0,24},{4,28},{8,16},{12,20},{16,8},{20,12},{24,0},{28,4},{1,25},{... | collective-permute-start | bytes 49160 | tf_op jit(solution)/shard_map/ppermute | solution.py:20
  91.9 4.9 %collective-permute-start.6 = (bf16[1,16,4,128]{3,1,0,2:T(8,128)(2,1)S(1)}, bf16[1,16,4,128]{3,1,0,2:T(8,128)(2,1)S(1)}, u32[]{:S(2)}, u32[]{:S(2)}) collective-permute-start(bf16[1,16,4,128]{3,1,0,2:T(8,128)(2,1)S(1)} %get-tuple-element.445), channel_id=1, source_target_pairs={{0,28},{4,24},{8,20},{12,16},{16,12},{20,8},{24,4},{28,0},{1,29},{... | collective-permute-start | bytes 49160 | tf_op jit(solution)/shard_map/ppermute | solution.py:20
  132.5 0.8 copy-start.7
